TPU v7x, 256 devices: a whole 4x4x8 slice. The times are simulated.
256 devices in a mesh: section: 2 (over core), seq: 16 (over x, y), exp: 8 (over z).
Axes of the slice: x: 4, y: 4, z: 8, core: 2. Of those that a mesh axis runs over, the one named last changes fastest.
Arguments:
- hidden_in: bfloat16 [2048, 2048], P('seq'), may hold values from -6 to 6
- seg_ids: int32 [2048], P('seq'), may hold values from 0 to 7, never falling along the last dimension, each value on 1 to 1024 neighbouring positions
- attn_gain: float32 [2048], replicated, may hold values from 0.25 to 1.75
- w_query: bfloat16 [2048, 2048], P(None, ('section', 'exp'))
- w_key: bfloat16 [2048, 2048], P(None, ('section', 'exp'))
- w_value: bfloat16 [2048, 2048], P(None, ('section', 'exp')), may hold values from -0.125 to 0.125
- w_out: bfloat16 [2048, 2048], P(('section', 'exp')), may hold values from -0.5 to 0.5
- moe_gain: float32 [2048], replicated, may hold values from 0.25 to 1.75
- expert_ids: int32 [2048, 8], P(('seq', 'exp')), may hold values from 0 to 63, all different within a row; in each aligned block of 16 rows (0 to 15, 16 to 31, ...) at most 4 rows name the same one
- route_weights: float32 [2048, 8], P(('seq', 'exp')), may hold values from 0.1 to 0.6
- gate_halves: bfloat16 [128, 2048, 512], P(('seq', 'exp'), None, 'section'), may hold values from -0.125 to 0.125
- up_halves: bfloat16 [128, 2048, 512], P(('seq', 'exp'), None, 'section'), may hold values from -0.125 to 0.125
- down_halves: bfloat16 [128, 512, 2048], P(('seq', 'exp'), 'section'), may hold values from -0.1875 to 0.1875
Outputs:
- layer_out: bfloat16 [2048, 2048], P(('seq', 'exp'))
Inputs may be any that keep to these rules, and one draw needn't show every extreme that they name: `seg_ids`: prompt numbers never fall along the batch; each prompt holds 1 to 1024 tokens, and one holds exactly 1024. `expert_ids`: A token's 8 experts are distinct. In each aligned block of 16 tokens (the tokens of one device along seq and exp), no expert is chosen by more than 4 of the block's tokens, a bound that some block reaches.
All inputs are finite; a program needn't handle non-finite values.
Results may differ from a plain program's by a relative error of at most 0.012.
Values may be sent and summed in bfloat16 or wider, within the bound.
No kernel may reach another device: no remote copies, remote signals or barrier semaphores. Data moves between devices by JAX's collectives and lax.ppermute only.
A program may use at most 64 MiB of HBM per device.

v0:
```python
import math
import jax
import jax.numpy as jnp
from jax import lax
from jax.sharding import PartitionSpec as P

epsilon = 1e-05
rope_base = 10000.0


def rms_scale(rows, gain):
    wide = rows.astype(jnp.float32)
    inverse = lax.rsqrt(jnp.mean(wide * wide, axis=-1, keepdims=True) + epsilon)
    return (wide * inverse * gain).astype(jnp.bfloat16)


def rotate(values, positions):
    half_dim = values.shape[-1] // 2
    frequency = rope_base ** (-2.0 * jnp.arange(half_dim, dtype=jnp.float32) / values.shape[-1])
    angles = positions.astype(jnp.float32)[:, None] * frequency[None, :]
    cosine = jnp.cos(angles)
    sine_part = jnp.sin(angles)
    first_half = values[:, :half_dim]
    second_half = values[:, half_dim:]
    return jnp.concatenate(
        [
            first_half * cosine - second_half * sine_part,
            second_half * cosine + first_half * sine_part,
        ],
        axis=-1,
    )


def per_device(
    hidden_in,
    seg_ids,
    attn_gain,
    w_query,
    w_key,
    w_value,
    w_out,
    moe_gain,
    expert_ids,
    route_weights,
    gate_halves,
    up_halves,
    down_halves,
):
    tok_seq = hidden_in.shape[0]
    width = hidden_in.shape[1]
    head_dim = w_query.shape[1]
    positions = lax.axis_index("seq") * tok_seq + jnp.arange(tok_seq, dtype=jnp.int32)
    normed = rms_scale(hidden_in, attn_gain)
    query_rows = rotate(
        jnp.dot(normed, w_query, preferred_element_type=jnp.float32), positions
    ).astype(jnp.bfloat16)
    key_rows = rotate(jnp.dot(normed, w_key, preferred_element_type=jnp.float32), positions).astype(
        jnp.bfloat16
    )
    value_rows = jnp.dot(normed, w_value, preferred_element_type=jnp.float32).astype(jnp.bfloat16)
    score_scale = 1.0 / math.sqrt(head_dim)
    run_max = jnp.full((tok_seq,), -1e30, jnp.float32)
    seg_block = jnp.broadcast_to(seg_ids.astype(jnp.bfloat16)[:, None], (tok_seq, head_dim))
    packed = jnp.concatenate([key_rows, value_rows, seg_block], axis=1)
    gathered = lax.all_gather(packed, "seq", axis=0, tiled=True)
    piece_keys = gathered[:, :head_dim]
    piece_values = gathered[:, head_dim : 2 * head_dim]
    key_segs = gathered[:, 2 * head_dim].astype(jnp.int32)
    piece_rows = piece_keys.shape[0]
    scores = (
        lax.dot_general(
            query_rows, piece_keys, (((1,), (1,)), ((), ())), preferred_element_type=jnp.float32
        )
        * score_scale
    )
    key_pos = jnp.arange(piece_rows, dtype=jnp.int32)
    allowed = (seg_ids[:, None] == key_segs[None, :]) & (key_pos[None, :] <= positions[:, None])
    masked = jnp.where(allowed, scores, -1e30)
    new_max = jnp.maximum(run_max, jnp.max(masked, axis=1))
    weights = jnp.where(allowed, jnp.exp(masked - new_max[:, None]), 0.0)
    run_total = jnp.sum(weights, axis=1)
    weighted_sum = jnp.dot(
        weights.astype(jnp.bfloat16), piece_values, preferred_element_type=jnp.float32
    )
    run_max, run_total, weighted_sum = (new_max, run_total, weighted_sum)
    head_out = (weighted_sum / run_total[:, None]).astype(jnp.bfloat16)
    partial_value = jnp.dot(head_out, w_out, preferred_element_type=jnp.float32)
    tok_dev = tok_seq // lax.axis_size("exp")
    own_start = lax.axis_index("exp") * tok_dev
    summed = lax.psum_scatter(partial_value, "exp", scatter_dimension=0, tiled=True)
    summed = summed + lax.ppermute(summed, "section", [(0, 1), (1, 0)])
    own_rows = lax.dynamic_slice_in_dim(hidden_in, own_start, tok_dev, 0)
    residual = (own_rows.astype(jnp.float32) + summed).astype(jnp.bfloat16)
    moe_in = rms_scale(residual, moe_gain)
    experts = lax.axis_size("seq") * lax.axis_size("exp") // 2
    top_count = expert_ids.shape[1]
    capacity = min(tok_dev, max(2, 2 * tok_dev * top_count // experts))
    row_count = tok_dev * top_count
    flat_ids = expert_ids.reshape(row_count)
    one_hot = (flat_ids[:, None] == jnp.arange(experts, dtype=jnp.int32)[None, :]).astype(jnp.int32)
    slot_rank = jnp.sum((jnp.cumsum(one_hot, axis=0) - one_hot) * one_hot, axis=1)
    slot_index = flat_ids * capacity + slot_rank
    placed = slot_index[:, None] == jnp.arange(experts * capacity, dtype=jnp.int32)[None, :]
    repeated = jnp.repeat(moe_in, top_count, axis=0)
    outgoing = lax.dot_general(
        placed.astype(jnp.bfloat16),
        repeated,
        (((0,), (0,)), ((), ())),
        preferred_element_type=jnp.float32,
    ).astype(jnp.bfloat16)
    row_token = jnp.arange(row_count, dtype=jnp.int32) // top_count
    token_hot = (row_token[None, :] == jnp.arange(tok_dev, dtype=jnp.int32)[:, None]).astype(
        jnp.float32
    )
    weighted = token_hot * route_weights.reshape(row_count)[None, :]
    combine = jnp.dot(weighted, placed.astype(jnp.float32), precision=lax.Precision.HIGHEST)
    doubled = jnp.broadcast_to(
        outgoing.reshape(experts, 1, capacity, width), (experts, 2, capacity, width)
    ).reshape(2 * experts, capacity, width)
    arrived = lax.all_to_all(doubled, ("seq", "exp"), split_axis=0, concat_axis=0, tiled=True)
    flat_rows = arrived.reshape(-1, width)
    gate_proj = jnp.dot(flat_rows, gate_halves[0], preferred_element_type=jnp.float32)
    up_proj = jnp.dot(flat_rows, up_halves[0], preferred_element_type=jnp.float32)
    activated = (jax.nn.silu(gate_proj) * up_proj).astype(jnp.bfloat16)
    returned = lax.all_to_all(
        jnp.dot(activated, down_halves[0], preferred_element_type=jnp.float32)
        .astype(jnp.bfloat16)
        .reshape(arrived.shape),
        ("seq", "exp"),
        split_axis=0,
        concat_axis=0,
        tiled=True,
    )
    halves_sum = jnp.sum(
        returned.reshape(experts, 2, capacity, width).astype(jnp.float32), axis=1
    ).reshape(experts * capacity, width)
    moe_part = jnp.dot(combine, halves_sum, precision=lax.Precision.HIGHEST)
    moe_total = moe_part + lax.ppermute(moe_part, "section", [(0, 1), (1, 0)])
    return (residual.astype(jnp.float32) + moe_total).astype(jnp.bfloat16)


def solution(mesh):
    in_specs = (
        P("seq", None),
        P("seq"),
        P(),
        P(None, ("section", "exp")),
        P(None, ("section", "exp")),
        P(None, ("section", "exp")),
        P(("section", "exp"), None),
        P(),
        P(("seq", "exp"), None),
        P(("seq", "exp"), None),
        P(("seq", "exp"), None, "section"),
        P(("seq", "exp"), None, "section"),
        P(("seq", "exp"), "section", None),
    )
    out_specs = P(("seq", "exp"), None)
    return jax.shard_map(
        per_device, mesh=mesh, in_specs=in_specs, out_specs=out_specs, check_vma=False
    )
```

profile of v0, /device:TPU:1, one launch (start us, length us, event | category | flops | bytes accessed | tf_op | source)
XLA Modules:
  0.0 270.6 jit_solution(9258952518360087763)
XLA Ops:
  6.5 0.0 all-gather.2.cloned.1.call-start
  6.6 0.0 copy-start.7
  6.6 1.4 fusion.4
  8.0 1.6 fusion.76
  9.6 1.6 fusion.79
  11.3 0.4 convolution_convert_fusion.2
  11.7 0.0 copy-start.3
  11.7 0.2 fusion.59
  12.0 0.6 pad_maximum_fusion
  12.6 0.0 all-gather.2.cloned.1.call-update
  12.6 0.0 reduce-scatter.2.cloned.1.call-start
  12.7 52.2 %all-gather.2.cloned.1.call-done = bf16[2048,384]{0,1:T(8,128)(2,1)} async-done(((bf16[128,384]{0,1:T(8,128)(2,1)}), bf16[2048,384]{0,1:T(8,128)(2,1)}) %all-gather.2.cloned.1.call-update) | async-done | bytes 1572880 | tf_op jit(solution)/shard_map/all_gather | solution.py:65
  64.9 0.8 slice_convert_fusion
  65.7 1.5 fusion.81
  67.2 0.5 fusion.13
  67.7 0.0 copy-start.5
  67.7 0.0 copy-start.4
  67.7 2.8 %fusion.3 = f32[128,2048]{1,0:T(8,128)} fusion(bf16[128,2048]{1,0:T(8,128)(2,1)S(1)} %copy-done.3, f32[128,2048]{1,0:T(8,128)S(1)} %get-tuple-element.14, bf16[2048,384]{0,1:T(8,128)(2,1)} %all-gather.2.cloned.1.call-done, f32[128]{0:T(128)S(1)} %broadcast_maximum_fusion, s32[128]{0:T(128)S(1)} %iota_add_fusion, s32[2048]{0:T(1024)S(1)} %bitcast.29, ...), kind=kOutput, calls=%fused_computation.12 | convolution fusion | flops 135823360 | bytes 3155968 | tf_op jit(solution)/shard_map/dot_general | solution.py:87
  70.6 0.0 reduce-scatter.2.cloned.1.call-update
  70.6 0.1 copy.17
  70.7 0.1 reshape.89
  70.8 0.1 fusion.45
  70.9 0.2 reduce_window_sum.11
  71.0 0.2 select_reduce_fusion
  71.2 35.1 %reduce-scatter.2.cloned.1.call-done = f32[16,2048]{1,0:T(8,128)} async-done(((f32[128,2048]{1,0:T(8,128)}), f32[16,2048]{1,0:T(8,128)}) %reduce-scatter.2.cloned.1.call-update) | async-done | bytes 131088 | tf_op jit(solution)/shard_map/reduce_scatter | solution.py:90
  106.3 5.2 %collective-permute-start = (f32[16,2048]{1,0:T(8,128)}, f32[16,2048]{1,0:T(8,128)S(1)}, u32[]{:S(2)}, u32[]{:S(2)}) collective-permute-start(f32[16,2048]{1,0:T(8,128)} %reduce-scatter.2.cloned.1.call-done), channel_id=1, source_target_pairs={{0,128},{128,0},{1,129},{129,1},{2,130},{130,2},{3,131},{131,3},{4... | collective-permute-start | bytes 393224 | tf_op jit(solution)/shard_map/ppermute | solution.py:91
  111.5 1.2 collective-permute-done
  112.7 1.0 fusion.38
  113.7 0.1 fusion.40
  113.8 0.5 convolution_convert_fusion.1
  114.4 0.4 broadcast_in_dim.22
  114.8 1.2 broadcast_in_dim.23
  116.0 63.8 %all_to_all.10 = bf16[128,4,2048]{2,1,0:T(4,128)(2,1)S(1)} all-to-all(bf16[128,4,2048]{2,1,0:T(4,128)(2,1)S(1)} %bitcast.26), channel_id=1, replica_groups=mesh['section'=2,'seq'=16,'exp'=8] {'seq','exp'}, dimensions={0} | all-to-all | bytes 4194304 | tf_op jit(solution)/shard_map/all_to_all | solution.py:120
  179.9 2.1 reshape.92
  181.9 3.5 %fusion.10 = f32[512,256]{1,0:T(8,128)} fusion(bf16[512,2048]{1,0:T(8,128)(2,1)} %reshape.92, bf16[1,2048,256]{2,1,0:T(8,128)(2,1)} %param.23), kind=kOutput, calls=%fused_computation.18 | convolution fusion | flops 536870912 | bytes 3670016 | tf_op jit(solution)/shard_map/dot_general | solution.py:122
  185.5 5.0 %convolution_convert_fusion = bf16[512,2048]{1,0:T(8,128)(2,1)} fusion(bf16[512,2048]{1,0:T(8,128)(2,1)S(1)} %copy-done.1, bf16[1,256,2048]{2,1,0:T(8,128)(2,1)S(1)} %copy-done, bf16[1,2048,256]{2,1,0:T(8,128)(2,1)} %param.24, f32[512,256]{1,0:T(8,128)} %fusion.10), kind=kOutput, calls=%fused_computation.1 | convolution fusion | flops 1075576832 | bytes 6815744 | tf_op jit(solution)/shard_map/dot_general | solution.py:126
  190.5 4.1 %reshape.93 = bf16[128,4,2048]{2,1,0:T(4,128)(2,1)} reshape(bf16[512,2048]{1,0:T(8,128)(2,1)} %convolution_convert_fusion) | data formatting | bytes 4194304 | tf_op jit(solution)/shard_map/reshape | solution.py:128
  194.6 6.5 %all-to-all-start.1 = ((bf16[128,4,2048]{2,1,0:T(4,128)(2,1)}), bf16[128,4,2048]{2,1,0:T(4,128)(2,1)S(1)}, u32[]{:S(2)}, u32[]{:S(2)}) async-start(bf16[128,4,2048]{2,1,0:T(4,128)(2,1)} %reshape.93), calls=%async_computation.2 | async-start | bytes 4194304 | tf_op jit(solution)/shard_map/all_to_all | solution.py:125
  201.1 0.1 copy.16
  201.2 0.1 mul.147
  201.3 0.2 fusion.42
  201.5 50.7 %all-to-all-done.1 = bf16[128,4,2048]{2,1,0:T(4,128)(2,1)S(1)} async-done(((bf16[128,4,2048]{2,1,0:T(4,128)(2,1)}), bf16[128,4,2048]{2,1,0:T(4,128)(2,1)S(1)}, u32[]{:S(2)}, u32[]{:S(2)}) %all-to-all-start.1) | async-done | bytes 2097184 | tf_op jit(solution)/shard_map/all_to_all | solution.py:125
  252.2 2.7 convert_reduce_fusion
  254.9 2.0 reshape.94
  256.8 1.1 fusion.82
  257.9 4.2 %collective-permute-start.1 = (f32[16,2048]{1,0:T(8,128)S(1)}, f32[16,2048]{1,0:T(8,128)S(1)}, u32[]{:S(2)}, u32[]{:S(2)}) collective-permute-start(f32[16,2048]{1,0:T(8,128)S(1)} %fusion.82), channel_id=1, source_target_pairs={{0,128},{128,0},{1,129},{129,1},{2,130},{130,2},{3,131},{131,3},{4... | collective-permute-start | bytes 393224 | tf_op jit(solution)/shard_map/ppermute | solution.py:138
  262.1 1.0 collective-permute-done.1
  263.1 0.7 fusion.41
  (26 shorter events, 0.1 us)
Async XLA Ops:
  6.5 178.9 %copy-start = (bf16[1,256,2048]{2,1,0:T(8,128)(2,1)S(1)}, bf16[1,256,2048]{2,1,0:T(8,128)(2,1)}, u32[]{:S(2)}) copy-start(bf16[1,256,2048]{2,1,0:T(8,128)(2,1)} %param.25) | copy-start | bytes 3145732
  6.5 4.7 %copy-start.2 = (bf16[128,2048]{1,0:T(8,128)(2,1)S(1)}, bf16[128,2048]{1,0:T(8,128)(2,1)}, u32[]{:S(2)}) copy-start(bf16[128,2048]{1,0:T(8,128)(2,1)} %param.13) | copy-start | bytes 1572868
  6.5 4.7 %copy-start.9 = (f32[2048]{0:T(1024)S(1)}, f32[2048]{0:T(1024)}, u32[]{:S(2)}) copy-start(f32[2048]{0:T(1024)} %param.15) | copy-start | bytes 24580
  6.5 4.7 %copy-start.8 = (bf16[2048,128]{1,0:T(8,128)(2,1)S(1)}, bf16[2048,128]{1,0:T(8,128)(2,1)}, u32[]{:S(2)}) copy-start(bf16[2048,128]{1,0:T(8,128)(2,1)} %param.18) | copy-start | bytes 1572868
  6.5 58.4 %all-gather.2.cloned.1.call-start = ((), (), s32[]{:S(2)}) async-start(), calls=%async_computation.3 | async-start | bytes 1671168 | tf_op jit(solution)/shard_map/all_gather | solution.py:65
  6.6 5.1 %copy-start.7 = (s32[128]{0:T(128)S(1)}, s32[128]{0:T(128)}, u32[]{:S(2)}) copy-start(s32[128]{0:T(128)} %param.14) | copy-start | bytes 1540
  11.7 56.0 %copy-start.3 = (bf16[128,2048]{1,0:T(8,128)(2,1)S(1)}, bf16[128,2048]{1,0:T(8,128)(2,1)}, u32[]{:S(2)}) copy-start(bf16[128,2048]{1,0:T(8,128)(2,1)} %param.19) | copy-start | bytes 1572868
  12.6 93.7 %reduce-scatter.2.cloned.1.call-start = ((), (), s32[]{:S(2)}) async-start(), calls=%async_computation.4 | async-start | bytes 1179648 | tf_op jit(solution)/shard_map/reduce_scatter | solution.py:90
  67.7 2.9 %copy-start.5 = (s32[16,8]{0,1:T(8,128)S(1)}, s32[16,8]{0,1:T(8,128)}, u32[]{:S(2)}) copy-start(s32[16,8]{0,1:T(8,128)} %param.21) | copy-start | bytes 1540
  67.7 46.0 %copy-start.4 = (f32[2048]{0:T(1024)S(1)}, f32[2048]{0:T(1024)}, u32[]{:S(2)}) copy-start(f32[2048]{0:T(1024)} %param.20) | copy-start | bytes 24580
  106.3 6.4 %collective-permute-start = (f32[16,2048]{1,0:T(8,128)}, f32[16,2048]{1,0:T(8,128)S(1)}, u32[]{:S(2)}, u32[]{:S(2)}) collective-permute-start(f32[16,2048]{1,0:T(8,128)} %reduce-scatter.2.cloned.1.call-done), channel_id=1, source_target_pairs={{0,128},{128,0},{1,129},{129,1},{2,130},{130,2},{3,131},{131,3},{4... | collective-permute-start | bytes 393224 | tf_op jit(solution)/shard_map/ppermute | solution.py:91
  181.9 3.5 %copy-start.1 = (bf16[512,2048]{1,0:T(8,128)(2,1)S(1)}, bf16[512,2048]{1,0:T(8,128)(2,1)}, u32[]{:S(2)}) copy-start(bf16[512,2048]{1,0:T(8,128)(2,1)} %reshape.92) | copy-start | bytes 6291460
  194.6 6.5 %copy-start.6 = (f32[16,8]{0,1:T(8,128)S(1)}, f32[16,8]{0,1:T(8,128)}, u32[]{:S(2)}) copy-start(f32[16,8]{0,1:T(8,128)} %param.22) | copy-start | bytes 1540
  194.6 57.6 %all-to-all-start.1 = ((bf16[128,4,2048]{2,1,0:T(4,128)(2,1)}), bf16[128,4,2048]{2,1,0:T(4,128)(2,1)S(1)}, u32[]{:S(2)}, u32[]{:S(2)}) async-start(bf16[128,4,2048]{2,1,0:T(4,128)(2,1)} %reshape.93), calls=%async_computation.2 | async-start | bytes 4194304 | tf_op jit(solution)/shard_map/all_to_all | solution.py:125
  257.9 5.2 %collective-permute-start.1 = (f32[16,2048]{1,0:T(8,128)S(1)}, f32[16,2048]{1,0:T(8,128)S(1)}, u32[]{:S(2)}, u32[]{:S(2)}) collective-permute-start(f32[16,2048]{1,0:T(8,128)S(1)} %fusion.82), channel_id=1, source_target_pairs={{0,128},{128,0},{1,129},{129,1},{2,130},{130,2},{3,131},{131,3},{4... | collective-permute-start | bytes 393224 | tf_op jit(solution)/shard_map/ppermute | solution.py:138
Sparse Core Ops, SparseCore 0:
  12.7 52.1 all-gather.1
  70.7 35.5 reduce-scatter.1
where the time goes:
time: 271 us
  waiting for transfers between devices  140 us (52%)
  blocking collectives  63.8 us (24%)
  matrix products  18.4 us (7%)
  starting transfers between devices  16 us (6%)
  between operations  13.7 us (5%)
  local copies, waits for them, and re-layouts  10.2 us (4%)
  other arithmetic  8.38 us (3%)
    all_to_all x1, blocking collectives, per_device(): lax.all_to_all(doubled, ('seq', 'exp'), split_axis=0, concat_axis=0, tile...  63.8 us
    all_gather x1, waiting for transfers between devices, per_device(): gathered = lax.all_gather(packed, 'seq', axis=0, tiled=True)  52.2 us
    all_to_all x1, waiting for transfers between devices, per_device(): lax.all_to_all(jnp.dot(activated, down_halves[0], preferred_element_type=...  50.7 us
    reduce_scatter x1, waiting for transfers between devices, per_device(): lax.psum_scatter(partial_value, 'exp', scatter_dimension=0, tiled=True)  35.1 us
    all_to_all x1, starting transfers between devices, per_device(): lax.all_to_all(jnp.dot(activated, down_halves[0], preferred_element_type=...  6.52 us
  transfers between devices with their start and end apart: 5, of which 5 were waited for; matrix products, arithmetic and copies ran while one was open for 0% of the time, Pallas kernels for 0%

commit v1 on v0

--- a/solution.py
+++ b/solution.py
@@ -62,7 +62,9 @@
     run_max = jnp.full((tok_seq,), -1e30, jnp.float32)
     seg_block = jnp.broadcast_to(seg_ids.astype(jnp.bfloat16)[:, None], (tok_seq, head_dim))
     packed = jnp.concatenate([key_rows, value_rows, seg_block], axis=1)
-    gathered = lax.all_gather(packed, "seq", axis=0, tiled=True)
+    gathered = jnp.concatenate(
+        lax.all_to_all(jnp.stack([packed] * lax.axis_size("seq")), "seq", 0, 0), axis=0
+    )
     piece_keys = gathered[:, :head_dim]
     piece_values = gathered[:, head_dim : 2 * head_dim]
     key_segs = gathered[:, 2 * head_dim].astype(jnp.int32)

time: 271 us -> 253 us (0.934)
  waiting for transfers between devices: 140 us -> 110 us
  starting transfers between devices: 16 us -> 24 us
  local copies, waits for them, and re-layouts: 10.2 us -> 13.2 us
    all_gather x1 -> x0, waiting for transfers between devices: 52.2 us -> none  [per_device(): gathered = lax.all_gather(packed, 'seq', axis=0, tiled=True)]
    all_to_all x0 -> x1, waiting for transfers between devices: none -> 20.7 us  [per_device(): lax.all_to_all(jnp.stack([packed] * lax.axis_size('seq')), 'seq', 0, 0)]
    all_to_all x0 -> x1, starting transfers between devices: none -> 7.58 us  [per_device(): lax.all_to_all(jnp.stack([packed] * lax.axis_size('seq')), 'seq', 0, 0)]
where the time goes in v1:
time: 253 us; the launch traced here: 252 us
  waiting for transfers between devices  110 us (43%)
  blocking collectives  63.9 us (25%)
  starting transfers between devices  24 us (9%)
  matrix products  18.3 us (7%)
  between operations  13.7 us (5%)
  local copies, waits for them, and re-layouts  13.2 us (5%)
  other arithmetic  8.46 us (3%)
    all_to_all x1, blocking collectives, per_device(): lax.all_to_all(doubled, ('seq', 'exp'), split_axis=0, concat_axis=0, tile...  63.9 us
    all_to_all x1, waiting for transfers between devices, per_device(): lax.all_to_all(jnp.dot(activated, down_halves[0], preferred_element_type=...  50.8 us
    reduce_scatter x1, waiting for transfers between devices, per_device(): lax.psum_scatter(partial_value, 'exp', scatter_dimension=0, tiled=True)  36.7 us
    all_to_all x1, waiting for transfers between devices, per_device(): lax.all_to_all(jnp.stack([packed] * lax.axis_size('seq')), 'seq', 0, 0)  20.7 us
    all_to_all x1, starting transfers between devices, per_device(): lax.all_to_all(jnp.stack([packed] * lax.axis_size('seq')), 'seq', 0, 0)  7.58 us
    all_to_all x1, starting transfers between devices, per_device(): lax.all_to_all(jnp.dot(activated, down_halves[0], preferred_element_type=...  6.52 us
    ppermute x1, starting transfers between devices, per_device(): summed = summed + lax.ppermute(summed, 'section', [(0, 1), (1, 0)])  5.63 us
  transfers between devices with their start and end apart: 5, of which 5 were waited for; matrix products, arithmetic and copies ran while one was open for 0% of the time, Pallas kernels for 0%

profile of v1, /device:TPU:1, one launch (start us, length us, event | category | flops | bytes accessed | tf_op | source)
XLA Modules:
  0.0 251.9 jit_solution(10548553380876669806)
XLA Ops:
  6.6 0.0 copy-start.7
  6.6 1.4 fusion.4
  7.9 1.6 fusion.76
  9.6 1.6 fusion.79
  11.3 0.4 convolution_convert_fusion.2
  11.7 0.0 copy-done.7
  11.7 0.2 fusion.59
  11.9 1.5 stack.2
  13.4 7.6 %all-to-all-start = ((bf16[16,128,384]{1,2,0:T(8,128)(2,1)}), bf16[16,128,384]{1,2,0:T(8,128)(2,1)S(1)}, u32[]{:S(2)}, u32[]{:S(2)}) async-start(bf16[16,128,384]{1,2,0:T(8,128)(2,1)} %stack.2), calls=%async_computation | async-start | bytes 3145728 | tf_op jit(solution)/shard_map/all_to_all | solution.py:66
  21.0 0.0 reduce-scatter.2.cloned.1.call-start
  21.0 20.7 %all-to-all-done = bf16[16,128,384]{1,2,0:T(8,128)(2,1)S(1)} async-done(((bf16[16,128,384]{1,2,0:T(8,128)(2,1)}), bf16[16,128,384]{1,2,0:T(8,128)(2,1)S(1)}, u32[]{:S(2)}, u32[]{:S(2)}) %all-to-all-start) | async-done | bytes 1572896 | tf_op jit(solution)/shard_map/all_to_all | solution.py:66
  41.7 1.6 copy.21
  43.3 1.4 convert_reduce_fusion.1
  44.7 1.6 fusion.81
  46.3 0.5 fusion.13
  46.8 0.0 copy-start.5
  46.8 0.0 copy-start.4
  46.8 2.7 %fusion.3 = f32[128,2048]{1,0:T(8,128)} fusion(bf16[128,2048]{1,0:T(8,128)(2,1)S(1)} %copy-done.3, f32[128,2048]{1,0:T(8,128)S(1)} %get-tuple-element.14, bf16[2048,384]{1,0:T(8,128)(2,1)} %bitcast.29, f32[128]{0:T(128)S(1)} %broadcast_maximum_fusion, s32[128]{0:T(128)S(1)} %iota_add_fusion, s32[2048]{0:T(1024)S(1)} %convert_reduce_fusion.1, ...), kind=kOutput, calls=%fused_computation.12 | convolution fusion | flops 135823360 | bytes 3155968 | tf_op jit(solution)/shard_map/dot_general | solution.py:89
  49.5 0.0 reduce-scatter.2.cloned.1.call-update
  49.5 0.1 copy.23
  49.6 0.1 reshape.95
  49.7 0.1 fusion.45
  49.8 0.2 reduce_window_sum.11
  50.0 0.2 select_reduce_fusion
  50.2 36.7 %reduce-scatter.2.cloned.1.call-done = f32[16,2048]{1,0:T(8,128)} async-done(((f32[128,2048]{1,0:T(8,128)}), f32[16,2048]{1,0:T(8,128)}) %reduce-scatter.2.cloned.1.call-update) | async-done | bytes 131088 | tf_op jit(solution)/shard_map/reduce_scatter | solution.py:92
  86.9 5.6 %collective-permute-start = (f32[16,2048]{1,0:T(8,128)}, f32[16,2048]{1,0:T(8,128)S(1)}, u32[]{:S(2)}, u32[]{:S(2)}) collective-permute-start(f32[16,2048]{1,0:T(8,128)} %reduce-scatter.2.cloned.1.call-done), channel_id=1, source_target_pairs={{0,128},{128,0},{1,129},{129,1},{2,130},{130,2},{3,131},{131,3},{4... | collective-permute-start | bytes 393224 | tf_op jit(solution)/shard_map/ppermute | solution.py:93
  92.5 1.2 collective-permute-done
  93.7 1.1 fusion.38
  94.8 0.1 fusion.40
  94.9 0.5 convolution_convert_fusion.1
  95.4 0.4 broadcast_in_dim.22
  95.8 1.2 broadcast_in_dim.23
  97.1 63.9 %all_to_all.15 = bf16[128,4,2048]{2,1,0:T(4,128)(2,1)S(1)} all-to-all(bf16[128,4,2048]{2,1,0:T(4,128)(2,1)S(1)} %bitcast.26), channel_id=1, replica_groups=mesh['section'=2,'seq'=16,'exp'=8] {'seq','exp'}, dimensions={0} | all-to-all | bytes 4194304 | tf_op jit(solution)/shard_map/all_to_all | solution.py:122
  161.0 2.1 reshape.98
  163.1 3.5 %fusion.10 = f32[512,256]{1,0:T(8,128)} fusion(bf16[512,2048]{1,0:T(8,128)(2,1)} %reshape.98, bf16[1,2048,256]{2,1,0:T(8,128)(2,1)} %param.23), kind=kOutput, calls=%fused_computation.18 | convolution fusion | flops 536870912 | bytes 3670016 | tf_op jit(solution)/shard_map/dot_general | solution.py:124
  166.6 5.0 %convolution_convert_fusion = bf16[512,2048]{1,0:T(8,128)(2,1)} fusion(bf16[512,2048]{1,0:T(8,128)(2,1)S(1)} %copy-done.1, bf16[1,256,2048]{2,1,0:T(8,128)(2,1)S(1)} %copy-done, bf16[1,2048,256]{2,1,0:T(8,128)(2,1)} %param.24, f32[512,256]{1,0:T(8,128)} %fusion.10), kind=kOutput, calls=%fused_computation.1 | convolution fusion | flops 1075576832 | bytes 6815744 | tf_op jit(solution)/shard_map/dot_general | solution.py:128
  171.6 4.1 %reshape.99 = bf16[128,4,2048]{2,1,0:T(4,128)(2,1)} reshape(bf16[512,2048]{1,0:T(8,128)(2,1)} %convolution_convert_fusion) | data formatting | bytes 4194304 | tf_op jit(solution)/shard_map/reshape | solution.py:130
  175.7 6.5 %all-to-all-start.2 = ((bf16[128,4,2048]{2,1,0:T(4,128)(2,1)}), bf16[128,4,2048]{2,1,0:T(4,128)(2,1)S(1)}, u32[]{:S(2)}, u32[]{:S(2)}) async-start(bf16[128,4,2048]{2,1,0:T(4,128)(2,1)} %reshape.99), calls=%async_computation.3 | async-start | bytes 4194304 | tf_op jit(solution)/shard_map/all_to_all | solution.py:127
  182.3 0.1 copy.22
  182.3 0.1 mul.147
  182.4 0.2 fusion.42
  182.6 50.8 %all-to-all-done.2 = bf16[128,4,2048]{2,1,0:T(4,128)(2,1)S(1)} async-done(((bf16[128,4,2048]{2,1,0:T(4,128)(2,1)}), bf16[128,4,2048]{2,1,0:T(4,128)(2,1)S(1)}, u32[]{:S(2)}, u32[]{:S(2)}) %all-to-all-start.2) | async-done | bytes 2097184 | tf_op jit(solution)/shard_map/all_to_all | solution.py:127
  233.5 2.7 %convert_reduce_fusion = f32[64,4,2048]{2,1,0:T(4,128)} fusion(bf16[128,4,2048]{2,1,0:T(4,128)(2,1)S(1)} %all-to-all-done.2), kind=kLoop, calls=%fused_computation | loop fusion | flops 1572864 | bytes 4194304 | tf_op jit(solution)/shard_map/reduce_sum | solution.py:136
  236.2 2.0 reshape.100
  238.1 1.1 fusion.82
  239.2 4.2 %collective-permute-start.1 = (f32[16,2048]{1,0:T(8,128)S(1)}, f32[16,2048]{1,0:T(8,128)S(1)}, u32[]{:S(2)}, u32[]{:S(2)}) collective-permute-start(f32[16,2048]{1,0:T(8,128)S(1)} %fusion.82), channel_id=1, source_target_pairs={{0,128},{128,0},{1,129},{129,1},{2,130},{130,2},{3,131},{131,3},{4... | collective-permute-start | bytes 393224 | tf_op jit(solution)/shard_map/ppermute | solution.py:140
  243.4 1.0 collective-permute-done.1
  244.4 0.7 fusion.41
  (27 shorter events, 0.1 us)
Async XLA Ops:
  6.5 160.0 %copy-start = (bf16[1,256,2048]{2,1,0:T(8,128)(2,1)S(1)}, bf16[1,256,2048]{2,1,0:T(8,128)(2,1)}, u32[]{:S(2)}) copy-start(bf16[1,256,2048]{2,1,0:T(8,128)(2,1)} %param.25) | copy-start | bytes 3145732
  6.5 4.7 %copy-start.2 = (bf16[128,2048]{1,0:T(8,128)(2,1)S(1)}, bf16[128,2048]{1,0:T(8,128)(2,1)}, u32[]{:S(2)}) copy-start(bf16[128,2048]{1,0:T(8,128)(2,1)} %param.13) | copy-start | bytes 1572868
  6.5 4.7 %copy-start.9 = (f32[2048]{0:T(1024)S(1)}, f32[2048]{0:T(1024)}, u32[]{:S(2)}) copy-start(f32[2048]{0:T(1024)} %param.15) | copy-start | bytes 24580
  6.5 4.7 %copy-start.8 = (bf16[2048,128]{1,0:T(8,128)(2,1)S(1)}, bf16[2048,128]{1,0:T(8,128)(2,1)}, u32[]{:S(2)}) copy-start(bf16[2048,128]{1,0:T(8,128)(2,1)} %param.18) | copy-start | bytes 1572868
  6.6 5.1 %copy-start.7 = (s32[128]{0:T(128)S(1)}, s32[128]{0:T(128)}, u32[]{:S(2)}) copy-start(s32[128]{0:T(128)} %param.14) | copy-start | bytes 1540
  13.4 28.3 %all-to-all-start = ((bf16[16,128,384]{1,2,0:T(8,128)(2,1)}), bf16[16,128,384]{1,2,0:T(8,128)(2,1)S(1)}, u32[]{:S(2)}, u32[]{:S(2)}) async-start(bf16[16,128,384]{1,2,0:T(8,128)(2,1)} %stack.2), calls=%async_computation | async-start | bytes 3145728 | tf_op jit(solution)/shard_map/all_to_all | solution.py:66
  21.0 65.9 %reduce-scatter.2.cloned.1.call-start = ((), (), s32[]{:S(2)}) async-start(), calls=%async_computation.4 | async-start | bytes 1179648 | tf_op jit(solution)/shard_map/reduce_scatter | solution.py:92
  43.3 3.5 %copy-start.3 = (bf16[128,2048]{1,0:T(8,128)(2,1)S(1)}, bf16[128,2048]{1,0:T(8,128)(2,1)}, u32[]{:S(2)}) copy-start(bf16[128,2048]{1,0:T(8,128)(2,1)} %param.19) | copy-start | bytes 1572868
  46.8 2.8 %copy-start.5 = (s32[16,8]{0,1:T(8,128)S(1)}, s32[16,8]{0,1:T(8,128)}, u32[]{:S(2)}) copy-start(s32[16,8]{0,1:T(8,128)} %param.21) | copy-start | bytes 1540
  46.8 48.0 %copy-start.4 = (f32[2048]{0:T(1024)S(1)}, f32[2048]{0:T(1024)}, u32[]{:S(2)}) copy-start(f32[2048]{0:T(1024)} %param.20) | copy-start | bytes 24580
  86.9 6.8 %collective-permute-start = (f32[16,2048]{1,0:T(8,128)}, f32[16,2048]{1,0:T(8,128)S(1)}, u32[]{:S(2)}, u32[]{:S(2)}) collective-permute-start(f32[16,2048]{1,0:T(8,128)} %reduce-scatter.2.cloned.1.call-done), channel_id=1, source_target_pairs={{0,128},{128,0},{1,129},{129,1},{2,130},{130,2},{3,131},{131,3},{4... | collective-permute-start | bytes 393224 | tf_op jit(solution)/shard_map/ppermute | solution.py:93
  163.1 3.5 %copy-start.1 = (bf16[512,2048]{1,0:T(8,128)(2,1)S(1)}, bf16[512,2048]{1,0:T(8,128)(2,1)}, u32[]{:S(2)}) copy-start(bf16[512,2048]{1,0:T(8,128)(2,1)} %reshape.98) | copy-start | bytes 6291460
  175.7 6.5 %copy-start.6 = (f32[16,8]{0,1:T(8,128)S(1)}, f32[16,8]{0,1:T(8,128)}, u32[]{:S(2)}) copy-start(f32[16,8]{0,1:T(8,128)} %param.22) | copy-start | bytes 1540
  175.7 57.8 %all-to-all-start.2 = ((bf16[128,4,2048]{2,1,0:T(4,128)(2,1)}), bf16[128,4,2048]{2,1,0:T(4,128)(2,1)S(1)}, u32[]{:S(2)}, u32[]{:S(2)}) async-start(bf16[128,4,2048]{2,1,0:T(4,128)(2,1)} %reshape.99), calls=%async_computation.3 | async-start | bytes 4194304 | tf_op jit(solution)/shard_map/all_to_all | solution.py:127
  239.2 5.2 %collective-permute-start.1 = (f32[16,2048]{1,0:T(8,128)S(1)}, f32[16,2048]{1,0:T(8,128)S(1)}, u32[]{:S(2)}, u32[]{:S(2)}) collective-permute-start(f32[16,2048]{1,0:T(8,128)S(1)} %fusion.82), channel_id=1, source_target_pairs={{0,128},{128,0},{1,129},{129,1},{2,130},{130,2},{3,131},{131,3},{4... | collective-permute-start | bytes 393224 | tf_op jit(solution)/shard_map/ppermute | solution.py:140
Sparse Core Ops, SparseCore 0:
  49.7 37.1 reduce-scatter.1
